TPU v7x, 32 devices: a whole 2x2x4 slice. The times are simulated.
32 devices in a mesh: tile: 2 (over y), dom: 4 (over x, core), view: 4 (over z).
Axes of the slice: x: 2, y: 2, z: 4, core: 2. Of those that a mesh axis runs over, the one named last changes fastest.
Arguments:
- estimate: float32 [128, 32, 256], P(('tile', 'dom')), parts along dimension 0, may hold values from 0.25 to 4
- observed: float32 [4, 128, 32, 256], P('view', ('tile', 'dom')), parts along dimension 1, may hold values from 0.5 to 8
- psf: float32 [4, 4, 3, 9], P('view'), may hold values from 0.02 to 1
- src_map: int32 [4, 16], replicated, may hold values from 0 to 15, as said below
- depth_band: int32 [4, 64], P('view'), may hold values from 0 to 3, as said below
Outputs:
- new_estimate: float32 [128, 32, 256], P(('tile', 'dom')), parts along dimension 0
There are 2 independent parts, one for each index of `tile`. A program takes and returns all parts, laid end to end along the dimension named above; an argument that names none is the same for every part. Nothing has to cross between parts.
Inputs may be any that keep to these rules, and one draw needn't show every extreme that they name: For each view src_map is a permutation of the 16 joined blocks, and the 4 camera blocks f * 4 to f * 4 + 3 show blocks of 4 different depth slabs, one of each. For each view depth_band never falls along depth; it is 0 at the first plane and 3 at the last.
All inputs are finite; a program needn't handle non-finite values.
Results may differ from a plain program's by a relative error of at most 0.0001.
Values sent between devices are 32-bit elements; how exact they have to be, the bound alone decides.
No kernel may reach another device: no remote copies, remote signals or barrier semaphores. Data moves between devices by JAX's collectives and lax.ppermute only.
A program may use at most 64 MiB of HBM per device.

v0:
```python
import jax
import jax.numpy as jnp
from jax import lax
from jax.sharding import PartitionSpec as P

RADIUS = 4
precise = lax.Precision.HIGHEST


def extended_2(shard, sides, width):
    for axis, dim in sides:
        size, length = (lax.axis_size(axis), shard.shape[dim])
        up = [(i, (i + 1) % size) for i in range(size - 1)]
        down = [(j, i) for i, j in up]
        last = lax.slice_in_dim(shard, length - width, length, axis=dim)
        initial = lax.slice_in_dim(shard, 0, width, axis=dim)
        before = lax.ppermute(last, axis, up)
        after = lax.ppermute(initial, axis, down)
        shard = jnp.concatenate([before, shard, after], axis=dim)
    return shard


def taps_along(field, taps, axis, flipped):
    tap_count = taps.shape[1]
    reach = (tap_count - 1) // 2
    length = field.shape[axis]
    widths = [(0, 0), (0, 0), (0, 0)]
    widths[axis] = (reach, reach)
    padded = jnp.pad(field, widths)
    total = jnp.zeros(field.shape, jnp.float32)
    for offset in range(tap_count):
        start = 2 * reach - offset if flipped else offset
        piece = lax.slice_in_dim(padded, start, start + length, axis=axis)
        total = total + taps[:, offset][:, None, None] * piece
    return total


def lateral_fwd(field, x_taps, y_taps):
    inner = taps_along(field, x_taps, 2, False)
    return taps_along(inner, y_taps, 1, False)


def lateral_back(field, x_taps, y_taps):
    inner = taps_along(field, y_taps, 1, True)
    return taps_along(inner, x_taps, 2, True)


def body(estimate, observed, psf, src_map, depth_band):
    plane_count, row_count, lane_count = estimate.shape
    block_count = lax.axis_size("dom")
    block_rows = row_count // block_count
    dom_index = lax.axis_index("dom")
    view_index = lax.axis_index("view")
    view_count = lax.axis_size("view")
    plane_start = dom_index * plane_count
    slot_ids = jnp.arange(block_count, dtype=jnp.int32)
    my_map = lax.dynamic_index_in_dim(src_map, view_index, 0, keepdims=False)
    grid_map = my_map.reshape(block_count, block_count)
    source_dev = grid_map // block_count
    source_slot = grid_map % block_count
    send_slot = jnp.sum(jnp.where(source_dev == dom_index, source_slot, 0), axis=1)
    blocks = estimate.reshape(plane_count, block_count, block_rows, lane_count)
    outgoing = jnp.take(blocks, send_slot, axis=1)
    arrived = lax.all_to_all(outgoing, "dom", split_axis=1, concat_axis=1, tiled=True)
    my_sources = lax.dynamic_index_in_dim(source_dev, dom_index, 0, keepdims=False)
    camera = jnp.take(arrived, my_sources, axis=1).reshape(plane_count, row_count, lane_count)
    kernels = psf[0]
    band_all = depth_band[0]
    total_planes = band_all.shape[0]
    reach = (kernels.shape[2] - 1) // 2
    ext_count = plane_count + 2 * reach
    ext_index = jnp.clip(
        plane_start - reach + jnp.arange(ext_count, dtype=jnp.int32), 0, total_planes - 1
    )
    band_ext = jnp.take(band_all, ext_index)
    band_own = lax.dynamic_slice_in_dim(band_all, plane_start, plane_count)
    x_own = jnp.take(kernels[:, 2], band_own, axis=0)
    y_own = jnp.take(kernels[:, 1], band_own, axis=0)
    lateral = lateral_fwd(camera, x_own, y_own)
    extended = extended_2(lateral, (("dom", 0),), RADIUS)
    z_pos = jnp.arange(plane_count, dtype=jnp.int32)[:, None]
    s_pos = jnp.arange(ext_count, dtype=jnp.int32)[None, :]
    fwd_tap = s_pos - z_pos
    fwd_valid = (fwd_tap >= 0) & (fwd_tap <= 2 * reach)
    taps_own = jnp.take(kernels[:, 0], band_own, axis=0)
    row_sel = jnp.broadcast_to(z_pos, (plane_count, ext_count))
    depth_fwd = jnp.where(fwd_valid, taps_own[row_sel, jnp.clip(fwd_tap, 0, 2 * reach)], 0.0)
    blurred = jnp.einsum("zs,syx->zyx", depth_fwd, extended, precision=precise)
    ratio_field = observed[0] / blurred
    ratio_ext = extended_2(ratio_field, (("dom", 0),), RADIUS)
    back_tap = z_pos - s_pos + 2 * reach
    back_valid = (back_tap >= 0) & (back_tap <= 2 * reach)
    taps_ext = jnp.take(kernels[:, 0], band_ext, axis=0)
    col_sel = jnp.broadcast_to(s_pos, (plane_count, ext_count))
    depth_back = jnp.where(back_valid, taps_ext[col_sel, jnp.clip(back_tap, 0, 2 * reach)], 0.0)
    zback = jnp.einsum("zs,syx->zyx", depth_back, ratio_ext, precision=precise)
    back = lateral_back(zback, x_own, y_own)
    dest_slot = jnp.sum(
        jnp.where(my_sources[None, :] == slot_ids[:, None], slot_ids[None, :], 0), axis=1
    )
    inverse_slot = jnp.sum(
        jnp.where(send_slot[None, :] == slot_ids[:, None], slot_ids[None, :], 0), axis=1
    )
    back_blocks = back.reshape(plane_count, block_count, block_rows, lane_count)
    returning = jnp.take(back_blocks, dest_slot, axis=1)
    returned = lax.all_to_all(returning, "dom", split_axis=1, concat_axis=1, tiled=True)
    log_corr = jnp.log(jnp.take(returned, inverse_slot, axis=1))
    log_total = lax.psum(log_corr, "view")
    updated = blocks * jnp.exp(log_total / view_count)
    return updated.reshape(plane_count, row_count, lane_count)


def solution(mesh):
    in_specs = (
        P(("tile", "dom"), None, None),
        P("view", ("tile", "dom"), None, None),
        P("view", None, None, None),
        P(),
        P("view", None),
    )
    out_specs = P(("tile", "dom"), None, None)
    return jax.shard_map(body, mesh=mesh, in_specs=in_specs, out_specs=out_specs, check_vma=False)
```

profile of v0, /device:TPU:0, one launch (start us, length us, event | category | flops | bytes accessed | tf_op | source)
XLA Modules:
  0.0 108.7 jit_solution(233660518752022189)
XLA Ops:
  6.5 0.0 copy-start
  6.5 0.7 copy-done
  7.2 0.1 reshape.184
  7.3 0.1 fusion.101
  7.5 0.1 select_reduce_fusion.1
  7.6 1.6 %gather_fusion.7 = f32[4,16,8,256]{3,2,1,0:T(8,128)S(1)} fusion(f32[16,4,8,256]{3,2,1,0:T(8,128)} %bitcast.51, s32[1024]{0:T(1024)S(1)} %pad_clamp_fusion.3), kind=kCustom, calls=%fused_computation.1.clone | custom fusion | bytes 1048592 | tf_op jit(solution)/shard_map/jit(_take)/gather | solution.py:63
  9.2 0.9 select_bitcast_fusion.2
  10.2 4.2 %all-to-all-start = ((f32[16,4,8,256]{3,2,0,1:T(8,128)}), f32[16,4,8,256]{3,2,0,1:T(8,128)S(1)}, u32[]{:S(2)}, u32[]{:S(2)}) async-start(f32[16,4,8,256]{3,2,0,1:T(8,128)} %select_bitcast_fusion.2), calls=%async_computation | async-start | bytes 1048576 | tf_op jit(solution)/shard_map/all_to_all | solution.py:64
  14.4 0.0 copy-start.1
  14.4 0.6 copy-done.1
  15.1 0.7 gather_fusion
  15.8 0.0 copy-start.3
  15.8 0.1 compare_and_fusion.4
  15.9 0.6 copy-done.3
  16.5 0.6 gather_fusion.6
  17.1 0.6 gather_fusion.4
  17.7 0.6 gather_fusion.5
  18.2 0.1 broadcast_select_fusion.1
  18.3 0.6 gather_fusion.1
  18.9 0.5 slice_reduce_fusion.16
  19.4 0.1 broadcast_select_fusion
  19.4 3.8 %all-to-all-done = f32[16,4,8,256]{3,2,0,1:T(8,128)S(1)} async-done(((f32[16,4,8,256]{3,2,0,1:T(8,128)}), f32[16,4,8,256]{3,2,0,1:T(8,128)S(1)}, u32[]{:S(2)}, u32[]{:S(2)}) %all-to-all-start) | async-done | bytes 524320 | tf_op jit(solution)/shard_map/all_to_all | solution.py:64
  23.3 0.6 gather_fusion.8
  23.9 0.1 select_bitcast_fusion.1
  24.0 0.2 copy.22
  24.1 1.2 %fusion.51 = f32[16,32,256]{2,0,1:T(8,128)S(1)} fusion(f32[16,32,256]{2,0,1:T(8,128)S(1)} %bitcast.53, f32[16]{0:T(128)S(1)} %get-tuple-element.52, f32[16]{0:T(128)S(1)} %get-tuple-element.51, f32[16]{0:T(128)S(1)} %get-tuple-element.50, f32[16]{0:T(128)S(1)} %get-tuple-element.49, f32[16]{0:T(128)S(1)} %get-tuple-element.48, f32[16]{0:T(128)S(1)} %get-tuple-element.47, ...), kind=kLoop, calls=%fused_computation.95 | loop fusion | flops 2228224 | bytes 1049152 | tf_op jit(solution)/shard_map/add | solution.py:34
  25.3 0.4 fusion.19
  25.7 1.3 %collective-permute-start = (f32[4,32,256]{2,0,1:T(4,128)S(1)}, f32[4,32,256]{2,0,1:T(4,128)S(1)}, u32[]{:S(2)}, u32[]{:S(2)}) collective-permute-start(f32[4,32,256]{2,0,1:T(4,128)S(1)} %get-tuple-element.33), channel_id=1, source_target_pairs={{0,4},{4,8},{8,12},{1,5},{5,9},{9,13},{2,6},{6,10},{10,14},{3,7},{... | collective-permute-start | bytes 393224 | tf_op jit(solution)/shard_map/ppermute | solution.py:17
  27.0 1.3 %collective-permute-start.1 = (f32[4,32,256]{2,0,1:T(4,128)S(1)}, f32[4,32,256]{2,0,1:T(4,128)S(1)}, u32[]{:S(2)}, u32[]{:S(2)}) collective-permute-start(f32[4,32,256]{2,0,1:T(4,128)S(1)} %get-tuple-element.34), channel_id=1, source_target_pairs={{4,0},{8,4},{12,8},{5,1},{9,5},{13,9},{6,2},{10,6},{14,10},{7,3},{... | collective-permute-start | bytes 393224 | tf_op jit(solution)/shard_map/ppermute | solution.py:18
  28.4 0.1 reshape.266
  28.4 0.0 copy-start.4
  28.4 2.9 %gather_fusion.3 = f32[384]{0:T(512)S(1)} fusion(f32[16,9]{1,0:T(8,128)S(1)} %get-tuple-element.38, s32[384]{0:T(512)S(1)} %reshape.266), kind=kCustom, calls=%fused_computation.10 | custom fusion | bytes 6144 | tf_op jit(solution)/shard_map/gather | solution.py:87
  31.3 0.1 reshape.269
  31.4 0.0 collective-permute-done
  31.5 0.0 collective-permute-done.1
  31.5 0.0 copy-done.4
  31.5 0.9 convolution_divide_fusion
  32.4 4.9 %collective-permute-start.2 = (f32[4,32,256]{2,0,1:T(4,128)S(1)}, f32[4,32,256]{2,0,1:T(4,128)S(1)}, u32[]{:S(2)}, u32[]{:S(2)}) collective-permute-start(f32[4,32,256]{2,0,1:T(4,128)S(1)} %get-tuple-element.31), channel_id=1, source_target_pairs={{0,4},{4,8},{8,12},{1,5},{5,9},{9,13},{2,6},{6,10},{10,14},{3,7},{... | collective-permute-start | bytes 393224 | tf_op jit(solution)/shard_map/ppermute | solution.py:17
  37.3 1.3 %collective-permute-start.3 = (f32[4,32,256]{2,0,1:T(4,128)S(1)}, f32[4,32,256]{2,0,1:T(4,128)S(1)}, u32[]{:S(2)}, u32[]{:S(2)}) collective-permute-start(f32[4,32,256]{2,0,1:T(4,128)S(1)} %get-tuple-element.32), channel_id=1, source_target_pairs={{4,0},{8,4},{12,8},{5,1},{9,5},{13,9},{6,2},{10,6},{14,10},{7,3},{... | collective-permute-start | bytes 393224 | tf_op jit(solution)/shard_map/ppermute | solution.py:18
  38.6 0.1 reshape.260
  38.7 2.9 %gather_fusion.2 = f32[384]{0:T(512)S(1)} fusion(f32[24,9]{1,0:T(8,128)S(1)} %broadcast_select_fusion, s32[384]{0:T(512)S(1)} %reshape.260), kind=kCustom, calls=%fused_computation.9 | custom fusion | bytes 6144 | tf_op jit(solution)/shard_map/gather | solution.py:95
  41.6 0.1 reshape.263
  41.7 0.1 select_reduce_fusion
  41.8 0.0 collective-permute-done.2
  41.8 0.0 collective-permute-done.3
  41.8 0.7 fusion.5
  42.5 0.3 fusion.35
  42.9 1.2 %fusion.67 = f32[16,32,256]{2,0,1:T(8,128)S(1)} fusion(f32[16,32,256]{2,0,1:T(8,128)S(1)} %fusion.35, f32[16]{0:T(128)S(1)} %get-tuple-element.52, f32[16]{0:T(128)S(1)} %get-tuple-element.51, f32[16]{0:T(128)S(1)} %get-tuple-element.50, f32[16]{0:T(128)S(1)} %get-tuple-element.49, f32[16]{0:T(128)S(1)} %get-tuple-element.48, f32[16]{0:T(128)S(1)} %get-tuple-element.47, ...), kind=kLoop, calls=%fused_computation.111 | loop fusion | flops 2228224 | bytes 1049152 | tf_op jit(solution)/shard_map/add | solution.py:34
  44.0 0.3 copy.23
  44.3 0.6 gather_fusion.9
  44.9 0.9 select_bitcast_fusion
  45.8 4.0 %all-to-all-start.1 = ((f32[16,4,8,256]{3,2,0,1:T(8,128)}), f32[16,4,8,256]{3,2,0,1:T(8,128)S(1)}, u32[]{:S(2)}, u32[]{:S(2)}) async-start(f32[16,4,8,256]{3,2,0,1:T(8,128)} %select_bitcast_fusion), calls=%async_computation.1 | async-start | bytes 1048576 | tf_op jit(solution)/shard_map/all_to_all | solution.py:106
  49.9 0.0 all-reduce.6.cloned.1.call-start
  49.9 8.8 %all-to-all-done.1 = f32[16,4,8,256]{3,2,0,1:T(8,128)S(1)} async-done(((f32[16,4,8,256]{3,2,0,1:T(8,128)}), f32[16,4,8,256]{3,2,0,1:T(8,128)S(1)}, u32[]{:S(2)}, u32[]{:S(2)}) %all-to-all-start.1) | async-done | bytes 524320 | tf_op jit(solution)/shard_map/all_to_all | solution.py:106
  58.7 0.6 gather_fusion.10
  59.3 0.9 bitcast_log_fusion
  60.3 0.0 copy-start.2
  60.3 0.0 all-reduce.6.cloned.1.call-update
  60.3 39.7 %all-reduce.6.cloned.1.call-done = f32[16,4,8,256]{3,2,1,0:T(8,128)} async-done(((f32[16,4,8,256]{3,2,1,0:T(8,128)}), f32[16,4,8,256]{3,2,1,0:T(8,128)}) %all-reduce.6.cloned.1.call-update) | async-done | bytes 524304 | tf_op jit(solution)/shard_map/psum | solution.py:108
  100.0 0.0 copy-done.2
  100.0 1.9 %multiply_bitcast_fusion = f32[16,32,256]{2,1,0:T(8,128)} fusion(f32[16,4,8,256]{3,2,1,0:T(8,128)} %all-reduce.6.cloned.1.call-done, f32[16,32,256]{2,1,0:T(8,128)S(1)} %copy-done.2), kind=kLoop, calls=%fused_computation.124 | loop fusion | flops 262144 | bytes 1572864 | tf_op jit(solution)/shard_map/reshape | solution.py:110
  (24 shorter events, 0.4 us)
Async XLA Ops:
  6.5 0.7 copy-start
  10.2 13.1 %all-to-all-start = ((f32[16,4,8,256]{3,2,0,1:T(8,128)}), f32[16,4,8,256]{3,2,0,1:T(8,128)S(1)}, u32[]{:S(2)}, u32[]{:S(2)}) async-start(f32[16,4,8,256]{3,2,0,1:T(8,128)} %select_bitcast_fusion.2), calls=%async_computation | async-start | bytes 1048576 | tf_op jit(solution)/shard_map/all_to_all | solution.py:64
  14.4 0.7 copy-start.1
  15.8 0.7 copy-start.3
  25.7 5.7 %collective-permute-start = (f32[4,32,256]{2,0,1:T(4,128)S(1)}, f32[4,32,256]{2,0,1:T(4,128)S(1)}, u32[]{:S(2)}, u32[]{:S(2)}) collective-permute-start(f32[4,32,256]{2,0,1:T(4,128)S(1)} %get-tuple-element.33), channel_id=1, source_target_pairs={{0,4},{4,8},{8,12},{1,5},{5,9},{9,13},{2,6},{6,10},{10,14},{3,7},{... | collective-permute-start | bytes 393224 | tf_op jit(solution)/shard_map/ppermute | solution.py:17
  27.0 4.4 %collective-permute-start.1 = (f32[4,32,256]{2,0,1:T(4,128)S(1)}, f32[4,32,256]{2,0,1:T(4,128)S(1)}, u32[]{:S(2)}, u32[]{:S(2)}) collective-permute-start(f32[4,32,256]{2,0,1:T(4,128)S(1)} %get-tuple-element.34), channel_id=1, source_target_pairs={{4,0},{8,4},{12,8},{5,1},{9,5},{13,9},{6,2},{10,6},{14,10},{7,3},{... | collective-permute-start | bytes 393224 | tf_op jit(solution)/shard_map/ppermute | solution.py:18
  28.4 3.0 %copy-start.4 = (f32[1,16,32,256]{3,2,1,0:T(8,128)S(1)}, f32[1,16,32,256]{3,2,1,0:T(8,128)}, u32[]{:S(2)}) copy-start(f32[1,16,32,256]{3,2,1,0:T(8,128)} %param.10) | copy-start | bytes 1572868
  32.4 9.4 %collective-permute-start.2 = (f32[4,32,256]{2,0,1:T(4,128)S(1)}, f32[4,32,256]{2,0,1:T(4,128)S(1)}, u32[]{:S(2)}, u32[]{:S(2)}) collective-permute-start(f32[4,32,256]{2,0,1:T(4,128)S(1)} %get-tuple-element.31), channel_id=1, source_target_pairs={{0,4},{4,8},{8,12},{1,5},{5,9},{9,13},{2,6},{6,10},{10,14},{3,7},{... | collective-permute-start | bytes 393224 | tf_op jit(solution)/shard_map/ppermute | solution.py:17
  37.3 4.5 %collective-permute-start.3 = (f32[4,32,256]{2,0,1:T(4,128)S(1)}, f32[4,32,256]{2,0,1:T(4,128)S(1)}, u32[]{:S(2)}, u32[]{:S(2)}) collective-permute-start(f32[4,32,256]{2,0,1:T(4,128)S(1)} %get-tuple-element.32), channel_id=1, source_target_pairs={{4,0},{8,4},{12,8},{5,1},{9,5},{13,9},{6,2},{10,6},{14,10},{7,3},{... | collective-permute-start | bytes 393224 | tf_op jit(solution)/shard_map/ppermute | solution.py:18
  45.8 12.8 %all-to-all-start.1 = ((f32[16,4,8,256]{3,2,0,1:T(8,128)}), f32[16,4,8,256]{3,2,0,1:T(8,128)S(1)}, u32[]{:S(2)}, u32[]{:S(2)}) async-start(f32[16,4,8,256]{3,2,0,1:T(8,128)} %select_bitcast_fusion), calls=%async_computation.1 | async-start | bytes 1048576 | tf_op jit(solution)/shard_map/all_to_all | solution.py:106
  49.9 50.1 %all-reduce.6.cloned.1.call-start = ((), (), s32[]{:S(2)}) async-start(), calls=%async_computation.2 | async-start | bytes 1048576 | tf_op jit(solution)/shard_map/psum | solution.py:108
  60.3 39.7 %copy-start.2 = (f32[16,32,256]{2,1,0:T(8,128)S(1)}, f32[16,32,256]{2,1,0:T(8,128)}, u32[]{:S(2)}) copy-start(f32[16,32,256]{2,1,0:T(8,128)} %param.9) | copy-start | bytes 1572868
Sparse Core Ops, SparseCore 0:
  60.4 39.5 all-reduce.5
where the time goes:
time: 109 us
  waiting for transfers between devices  52.3 us (48%)
  starting transfers between devices  17 us (16%)
  local copies, waits for them, and re-layouts  15.6 us (14%)
  between operations  13.7 us (13%)
  other arithmetic  8.56 us (8%)
  matrix products  1.56 us (1%)
    psum x1, waiting for transfers between devices, body(): log_total = lax.psum(log_corr, 'view')  39.7 us
    all_to_all x1, waiting for transfers between devices, body(): lax.all_to_all(returning, 'dom', split_axis=1, concat_axis=1, tiled=True)  8.78 us
    ppermute x2, starting transfers between devices, extended_2(): before = lax.ppermute(last, axis, up)  6.17 us
    all_to_all x1, starting transfers between devices, body(): lax.all_to_all(outgoing, 'dom', split_axis=1, concat_axis=1, tiled=True)  4.24 us
    all_to_all x1, starting transfers between devices, body(): lax.all_to_all(returning, 'dom', split_axis=1, concat_axis=1, tiled=True)  4.03 us
    all_to_all x1, waiting for transfers between devices, body(): lax.all_to_all(outgoing, 'dom', split_axis=1, concat_axis=1, tiled=True)  3.78 us
    add x4, other arithmetic, taps_along(): total = total + taps[:, offset][:, None, None] * piece  3.03 us
    gather x2, local copies, waits for them, and re-layouts, body(): taps_ext[col_sel, jnp.clip(back_tap, 0, 2 * reach)]  2.96 us
  transfers between devices with their start and end apart: 7, of which 3 were waited for; matrix products, arithmetic and copies ran while one was open for 9% of the time, Pallas kernels for 0%

commit v1 on v0

--- a/solution.py
+++ b/solution.py
@@ -105,7 +105,8 @@
     returning = jnp.take(back_blocks, dest_slot, axis=1)
     returned = lax.all_to_all(returning, "dom", split_axis=1, concat_axis=1, tiled=True)
     log_corr = jnp.log(jnp.take(returned, inverse_slot, axis=1))
-    log_total = lax.psum(log_corr, "view")
+    parts = lax.all_gather(log_corr, "view", axis=0, tiled=False)
+    log_total = parts.sum(axis=0)
     updated = blocks * jnp.exp(log_total / view_count)
     return updated.reshape(plane_count, row_count, lane_count)
 

time: 109 us -> 117 us (1.073)
  waiting for transfers between devices: 52.3 us -> 60.6 us
  local copies, waits for them, and re-layouts: 15.6 us -> 14 us
  other arithmetic: 8.56 us -> 9.75 us
    all_gather x0 -> x1, waiting for transfers between devices: none -> 46.8 us  [body(): parts = lax.all_gather(log_corr, 'view', axis=0, tiled=False)]
    psum x1 -> x0, waiting for transfers between devices: 39.7 us -> none  [body(): log_total = lax.psum(log_corr, 'view')]
    reshape x1 -> x0, other arithmetic: 1.93 us -> none  [body(): return updated.reshape(plane_count, row_count, lane_count)]
    reduce_sum x0 -> x1, other arithmetic: none -> 1.9 us  [body(): log_total = parts.sum(axis=0)]
    unnamed x10, local copies, waits for them, and re-layouts: 1.94 us -> 0.69 us
    all_to_all x1, waiting for transfers between devices: 3.78 us -> 5.01 us  [body(): lax.all_to_all(outgoing, 'dom', split_axis=1, concat_axis=1, tiled=True)]
where the time goes in v1:
time: 117 us
  waiting for transfers between devices  60.6 us (52%)
  starting transfers between devices  17 us (15%)
  local copies, waits for them, and re-layouts  14 us (12%)
  between operations  13.8 us (12%)
  other arithmetic  9.75 us (8%)
  matrix products  1.53 us (1%)
    all_gather x1, waiting for transfers between devices, body(): parts = lax.all_gather(log_corr, 'view', axis=0, tiled=False)  46.8 us
    all_to_all x1, waiting for transfers between devices, body(): lax.all_to_all(returning, 'dom', split_axis=1, concat_axis=1, tiled=True)  8.78 us
    ppermute x2, starting transfers between devices, extended_2(): before = lax.ppermute(last, axis, up)  6.17 us
    all_to_all x1, waiting for transfers between devices, body(): lax.all_to_all(outgoing, 'dom', split_axis=1, concat_axis=1, tiled=True)  5.01 us
    all_to_all x1, starting transfers between devices, body(): lax.all_to_all(outgoing, 'dom', split_axis=1, concat_axis=1, tiled=True)  4.24 us
    all_to_all x1, starting transfers between devices, body(): lax.all_to_all(returning, 'dom', split_axis=1, concat_axis=1, tiled=True)  4.03 us
    add x4, other arithmetic, taps_along(): total = total + taps[:, offset][:, None, None] * piece  3.03 us
    gather x2, local copies, waits for them, and re-layouts, body(): taps_own[row_sel, jnp.clip(fwd_tap, 0, 2 * reach)]  2.96 us
  transfers between devices with their start and end apart: 7, of which 3 were waited for; matrix products, arithmetic and copies ran while one was open for 9% of the time, Pallas kernels for 0%

profile of v1, /device:TPU:0, one launch (start us, length us, event | category | flops | bytes accessed | tf_op | source)
XLA Modules:
  0.0 116.7 jit_solution(12324306947393694395)
XLA Ops:
  6.5 0.0 copy-start
  6.5 0.0 copy-start.1
  6.5 0.0 copy-start.3
  6.5 0.7 copy-done
  7.2 0.1 reshape.186
  7.3 0.1 fusion.101
  7.5 0.1 select_reduce_fusion.1
  7.6 1.6 %gather_fusion.7 = f32[4,16,8,256]{3,2,1,0:T(8,128)S(1)} fusion(f32[16,4,8,256]{3,2,1,0:T(8,128)} %bitcast.51, s32[1024]{0:T(1024)S(1)} %pad_clamp_fusion.3), kind=kCustom, calls=%fused_computation.1.clone | custom fusion | bytes 1048592 | tf_op jit(solution)/shard_map/jit(_take)/gather | solution.py:63
  9.2 0.9 select_bitcast_fusion.2
  10.2 4.2 %all-to-all-start = ((f32[16,4,8,256]{3,2,0,1:T(8,128)}), f32[16,4,8,256]{3,2,0,1:T(8,128)S(1)}, u32[]{:S(2)}, u32[]{:S(2)}) async-start(f32[16,4,8,256]{3,2,0,1:T(8,128)} %select_bitcast_fusion.2), calls=%async_computation | async-start | bytes 1048576 | tf_op jit(solution)/shard_map/all_to_all | solution.py:64
  14.4 0.0 copy-done.1
  14.4 0.7 gather_fusion
  15.2 0.1 compare_and_fusion.4
  15.3 0.0 copy-done.3
  15.3 0.6 gather_fusion.5
  15.9 0.6 gather_fusion.4
  16.4 0.6 gather_fusion.6
  17.0 0.1 broadcast_select_fusion.1
  17.1 0.6 gather_fusion.1
  17.6 0.5 slice_reduce_fusion.16
  18.1 0.1 broadcast_select_fusion
  18.2 5.0 %all-to-all-done = f32[16,4,8,256]{3,2,0,1:T(8,128)S(1)} async-done(((f32[16,4,8,256]{3,2,0,1:T(8,128)}), f32[16,4,8,256]{3,2,0,1:T(8,128)S(1)}, u32[]{:S(2)}, u32[]{:S(2)}) %all-to-all-start) | async-done | bytes 524320 | tf_op jit(solution)/shard_map/all_to_all | solution.py:64
  23.3 0.6 gather_fusion.8
  23.9 0.1 select_bitcast_fusion.1
  24.0 0.2 copy.14
  24.1 1.2 fusion.51
  25.3 0.4 fusion.19
  25.7 1.3 %collective-permute-start = (f32[4,32,256]{2,0,1:T(4,128)S(1)}, f32[4,32,256]{2,0,1:T(4,128)S(1)}, u32[]{:S(2)}, u32[]{:S(2)}) collective-permute-start(f32[4,32,256]{2,0,1:T(4,128)S(1)} %get-tuple-element.33), channel_id=1, source_target_pairs={{0,4},{4,8},{8,12},{1,5},{5,9},{9,13},{2,6},{6,10},{10,14},{3,7},{... | collective-permute-start | bytes 393224 | tf_op jit(solution)/shard_map/ppermute | solution.py:17
  27.0 1.3 %collective-permute-start.1 = (f32[4,32,256]{2,0,1:T(4,128)S(1)}, f32[4,32,256]{2,0,1:T(4,128)S(1)}, u32[]{:S(2)}, u32[]{:S(2)}) collective-permute-start(f32[4,32,256]{2,0,1:T(4,128)S(1)} %get-tuple-element.34), channel_id=1, source_target_pairs={{4,0},{8,4},{12,8},{5,1},{9,5},{13,9},{6,2},{10,6},{14,10},{7,3},{... | collective-permute-start | bytes 393224 | tf_op jit(solution)/shard_map/ppermute | solution.py:18
  28.3 0.1 reshape.267
  28.4 0.0 copy-start.4
  28.4 2.9 %gather_fusion.3 = f32[384]{0:T(512)S(1)} fusion(f32[16,9]{1,0:T(8,128)S(1)} %get-tuple-element.38, s32[384]{0:T(512)S(1)} %reshape.267), kind=kCustom, calls=%fused_computation.10 | custom fusion | bytes 6144 | tf_op jit(solution)/shard_map/gather | solution.py:87
  31.3 0.1 reshape.270
  31.4 0.0 collective-permute-done
  31.5 0.0 collective-permute-done.1
  31.5 0.0 copy-done.4
  31.5 0.9 convolution_divide_fusion
  32.4 4.9 %collective-permute-start.2 = (f32[4,32,256]{2,0,1:T(4,128)S(1)}, f32[4,32,256]{2,0,1:T(4,128)S(1)}, u32[]{:S(2)}, u32[]{:S(2)}) collective-permute-start(f32[4,32,256]{2,0,1:T(4,128)S(1)} %get-tuple-element.31), channel_id=1, source_target_pairs={{0,4},{4,8},{8,12},{1,5},{5,9},{9,13},{2,6},{6,10},{10,14},{3,7},{... | collective-permute-start | bytes 393224 | tf_op jit(solution)/shard_map/ppermute | solution.py:17
  37.3 1.3 %collective-permute-start.3 = (f32[4,32,256]{2,0,1:T(4,128)S(1)}, f32[4,32,256]{2,0,1:T(4,128)S(1)}, u32[]{:S(2)}, u32[]{:S(2)}) collective-permute-start(f32[4,32,256]{2,0,1:T(4,128)S(1)} %get-tuple-element.32), channel_id=1, source_target_pairs={{4,0},{8,4},{12,8},{5,1},{9,5},{13,9},{6,2},{10,6},{14,10},{7,3},{... | collective-permute-start | bytes 393224 | tf_op jit(solution)/shard_map/ppermute | solution.py:18
  38.6 0.1 reshape.261
  38.7 2.9 %gather_fusion.2 = f32[384]{0:T(512)S(1)} fusion(f32[24,9]{1,0:T(8,128)S(1)} %broadcast_select_fusion, s32[384]{0:T(512)S(1)} %reshape.261), kind=kCustom, calls=%fused_computation.9 | custom fusion | bytes 6144 | tf_op jit(solution)/shard_map/gather | solution.py:95
  41.6 0.1 reshape.264
  41.7 0.1 select_reduce_fusion
  41.8 0.0 collective-permute-done.2
  41.8 0.0 collective-permute-done.3
  41.8 0.6 fusion.5
  42.5 0.3 fusion.35
  42.8 1.2 fusion.67
  44.0 0.6 gather_fusion.9
  44.6 0.9 select_bitcast_fusion
  45.5 4.0 %all-to-all-start.1 = ((f32[16,4,8,256]{3,0,2,1:T(8,128)}), f32[16,4,8,256]{3,0,2,1:T(8,128)S(1)}, u32[]{:S(2)}, u32[]{:S(2)}) async-start(f32[16,4,8,256]{3,0,2,1:T(8,128)} %select_bitcast_fusion), calls=%async_computation.1 | async-start | bytes 1048576 | tf_op jit(solution)/shard_map/all_to_all | solution.py:106
  49.6 0.0 all-gather.3.cloned.1.call-start
  49.6 8.8 %all-to-all-done.1 = f32[16,4,8,256]{3,0,2,1:T(8,128)S(1)} async-done(((f32[16,4,8,256]{3,0,2,1:T(8,128)}), f32[16,4,8,256]{3,0,2,1:T(8,128)S(1)}, u32[]{:S(2)}, u32[]{:S(2)}) %all-to-all-start.1) | async-done | bytes 524320 | tf_op jit(solution)/shard_map/all_to_all | solution.py:106
  58.4 0.6 gather_fusion.10
  59.0 0.9 bitcast_log_fusion
  59.9 0.0 copy-start.2
  59.9 0.0 all-gather.3.cloned.1.call-update
  59.9 46.8 %all-gather.3.cloned.1.call-done = f32[64,4,8,256]{3,0,2,1:T(8,128)} async-done(((f32[16,4,8,256]{3,0,2,1:T(8,128)}), f32[64,4,8,256]{3,0,2,1:T(8,128)}) %all-gather.3.cloned.1.call-update) | async-done | bytes 2097168 | tf_op jit(solution)/shard_map/all_gather | solution.py:108
  106.7 1.9 %reduce_sum.39 = f32[16,4,8,256]{3,0,2,1:T(8,128)S(1)} reduce(f32[4,16,4,8,256]{4,1,0,3,2:T(8,128)} %bitcast.52, f32[]{:T(128)} %constant.110.clone.1), dimensions={0}, to_apply=%region_3.6 | reduce | flops 393216 | bytes 2621444 | tf_op jit(solution)/shard_map/reduce_sum | solution.py:109
  108.6 0.1 multiply_exponential_fusion
  108.7 0.0 copy-done.2
  108.7 1.1 copy_multiply_fusion
  (23 shorter events, 0.3 us)
Async XLA Ops:
  6.5 0.7 copy-start
  6.5 7.9 %copy-start.1 = (s32[1,64]{1,0:T(1,128)S(1)}, s32[1,64]{1,0:T(1,128)}, u32[]{:S(2)}) copy-start(s32[1,64]{1,0:T(1,128)} %param.13) | copy-start | bytes 772
  6.5 8.7 %copy-start.3 = (f32[1,4,3,9]{3,1,2,0:T(4,128)S(1)}, f32[1,4,3,9]{3,1,2,0:T(4,128)}, u32[]{:S(2)}) copy-start(f32[1,4,3,9]{3,1,2,0:T(4,128)} %param.11) | copy-start | bytes 1300
  10.2 13.1 %all-to-all-start = ((f32[16,4,8,256]{3,2,0,1:T(8,128)}), f32[16,4,8,256]{3,2,0,1:T(8,128)S(1)}, u32[]{:S(2)}, u32[]{:S(2)}) async-start(f32[16,4,8,256]{3,2,0,1:T(8,128)} %select_bitcast_fusion.2), calls=%async_computation | async-start | bytes 1048576 | tf_op jit(solution)/shard_map/all_to_all | solution.py:64
  25.7 5.7 %collective-permute-start = (f32[4,32,256]{2,0,1:T(4,128)S(1)}, f32[4,32,256]{2,0,1:T(4,128)S(1)}, u32[]{:S(2)}, u32[]{:S(2)}) collective-permute-start(f32[4,32,256]{2,0,1:T(4,128)S(1)} %get-tuple-element.33), channel_id=1, source_target_pairs={{0,4},{4,8},{8,12},{1,5},{5,9},{9,13},{2,6},{6,10},{10,14},{3,7},{... | collective-permute-start | bytes 393224 | tf_op jit(solution)/shard_map/ppermute | solution.py:17
  27.0 4.4 %collective-permute-start.1 = (f32[4,32,256]{2,0,1:T(4,128)S(1)}, f32[4,32,256]{2,0,1:T(4,128)S(1)}, u32[]{:S(2)}, u32[]{:S(2)}) collective-permute-start(f32[4,32,256]{2,0,1:T(4,128)S(1)} %get-tuple-element.34), channel_id=1, source_target_pairs={{4,0},{8,4},{12,8},{5,1},{9,5},{13,9},{6,2},{10,6},{14,10},{7,3},{... | collective-permute-start | bytes 393224 | tf_op jit(solution)/shard_map/ppermute | solution.py:18
  28.4 3.0 %copy-start.4 = (f32[1,16,32,256]{3,2,1,0:T(8,128)S(1)}, f32[1,16,32,256]{3,2,1,0:T(8,128)}, u32[]{:S(2)}) copy-start(f32[1,16,32,256]{3,2,1,0:T(8,128)} %param.10) | copy-start | bytes 1572868
  32.4 9.4 %collective-permute-start.2 = (f32[4,32,256]{2,0,1:T(4,128)S(1)}, f32[4,32,256]{2,0,1:T(4,128)S(1)}, u32[]{:S(2)}, u32[]{:S(2)}) collective-permute-start(f32[4,32,256]{2,0,1:T(4,128)S(1)} %get-tuple-element.31), channel_id=1, source_target_pairs={{0,4},{4,8},{8,12},{1,5},{5,9},{9,13},{2,6},{6,10},{10,14},{3,7},{... | collective-permute-start | bytes 393224 | tf_op jit(solution)/shard_map/ppermute | solution.py:17
  37.3 4.5 %collective-permute-start.3 = (f32[4,32,256]{2,0,1:T(4,128)S(1)}, f32[4,32,256]{2,0,1:T(4,128)S(1)}, u32[]{:S(2)}, u32[]{:S(2)}) collective-permute-start(f32[4,32,256]{2,0,1:T(4,128)S(1)} %get-tuple-element.32), channel_id=1, source_target_pairs={{4,0},{8,4},{12,8},{5,1},{9,5},{13,9},{6,2},{10,6},{14,10},{7,3},{... | collective-permute-start | bytes 393224 | tf_op jit(solution)/shard_map/ppermute | solution.py:18
  45.5 12.8 %all-to-all-start.1 = ((f32[16,4,8,256]{3,0,2,1:T(8,128)}), f32[16,4,8,256]{3,0,2,1:T(8,128)S(1)}, u32[]{:S(2)}, u32[]{:S(2)}) async-start(f32[16,4,8,256]{3,0,2,1:T(8,128)} %select_bitcast_fusion), calls=%async_computation.1 | async-start | bytes 1048576 | tf_op jit(solution)/shard_map/all_to_all | solution.py:106
  49.6 57.2 %all-gather.3.cloned.1.call-start = ((), (), s32[]{:S(2)}) async-start(), calls=%async_computation.2 | async-start | bytes 2621440 | tf_op jit(solution)/shard_map/all_gather | solution.py:108
  59.9 48.8 %copy-start.2 = (f32[16,32,256]{2,1,0:T(8,128)S(1)}, f32[16,32,256]{2,1,0:T(8,128)}, u32[]{:S(2)}) copy-start(f32[16,32,256]{2,1,0:T(8,128)} %param.9) | copy-start | bytes 1572868
Sparse Core Ops, SparseCore 0:
  60.0 46.6 all-gather.2
